TPU v7x, 512 devices: a whole 4x4x16 slice. The times are simulated.
512 devices in a mesh: blk: 32 (over z, y_lo), rep: 16 (over x, y_hi, core).
Axes of the slice: x: 4, y: 4 (y_hi: 2, y_lo: 2; y = y_hi * 2 + y_lo), z: 16, core: 2. Of those that a mesh axis runs over, the one named last changes fastest.
Arguments:
- feats: bfloat16 [32768, 256], P(('blk', 'rep')), may hold values from -6 to 6
- weight: bfloat16 [256, 256], replicated, may hold values from -0.375 to 0.375
- bias: float32 [256], replicated, may hold values from -4 to 4
- grad_out: bfloat16 [32768, 256], P(('blk', 'rep')), may hold values from -6 to 6
- tile_values: bfloat16 [32, 16, 2, 64, 128, 128], P('blk', 'rep'), may hold values from -0.03125 to 0.03125
- tile_rows: int32 [32, 16, 2, 64], P('blk', 'rep'), may hold values from 0 to 7, as said below
- tile_cols: int32 [32, 16, 2, 64], P('blk', 'rep'), may hold values from 0 to 7, as said below
- tile_count: int32 [32, 16, 2], P('blk', 'rep'), may hold values from 32 to 64, as said below
Outputs:
- out: bfloat16 [32768, 256], P(('blk', 'rep'))
- grad_feats: bfloat16 [32768, 256], P(('blk', 'rep'))
- grad_weight: float32 [256, 256], P('rep')
- grad_bias: float32 [256], replicated
Inputs may be any that keep to these rules, and one draw needn't show every extreme that they name: `tile_count`: some pair slot of some device holds exactly 64 live entries; slots past the count hold values that must be ignored. Within one pair slot the 64 entries name distinct (tile_rows, tile_cols) cells. `tile_cols`: see tile_rows: cells of one slot are distinct.
All inputs are finite; a program needn't handle non-finite values.
Results may differ from a plain program's by a relative error of at most 0.018.
Values may be sent and summed in bfloat16 or wider, within the bound.
No kernel may reach another device: no remote copies, remote signals or barrier semaphores. Data moves between devices by JAX's collectives and lax.ppermute only.
A program may use at most 64 MiB of HBM per device.

v0:
```python
import jax
import jax.numpy as jnp
from jax import lax
from jax.sharding import PartitionSpec as P


def passed_along(x, axis, by):
    devices = lax.axis_size(axis)
    return lax.ppermute(x, axis, [(i, (i + by) % devices) for i in range(devices)])


def dense_adjacency(tile_vals, tile_row, tile_col, live, tiles_per_part):
    entries, tile_size, _ = tile_vals.shape
    cells = tiles_per_part * tiles_per_part
    cell_of_entry = tile_row * tiles_per_part + tile_col
    alive = jnp.arange(entries) < live
    select = (cell_of_entry[None, :] == jnp.arange(cells)[:, None]) & alive[None, :]
    placed = jnp.dot(
        select.astype(tile_vals.dtype),
        tile_vals.reshape(entries, tile_size * tile_size),
        preferred_element_type=jnp.float32,
    ).astype(tile_vals.dtype)
    placed = placed.reshape(tiles_per_part, tiles_per_part, tile_size, tile_size)
    side = tiles_per_part * tile_size
    return placed.transpose(0, 2, 1, 3).reshape(side, side)


def activation(pre_act, cotangent):
    logistic = jax.nn.sigmoid(pre_act)
    result = (pre_act * logistic).astype(jnp.bfloat16)
    grad_pre = (
        cotangent.astype(jnp.float32) * logistic * (1.0 + pre_act * (1.0 - logistic))
    ).astype(jnp.bfloat16)
    return (result, grad_pre)


def body(feats, weight, bias, grad_out, tile_values, tile_rows, tile_cols, tile_count):
    replicas = lax.axis_size("rep")
    rep_index = lax.axis_index("rep")
    tile_size = tile_values.shape[-1]
    pair_slots = tile_values.shape[2]
    digit_count = (replicas - 1).bit_length()
    values_here = tile_values[0, 0]
    rows_here = tile_rows[0, 0]
    cols_here = tile_cols[0, 0]
    counts_here = tile_count[0, 0]
    hw_slice = jnp.dot(feats, weight, preferred_element_type=jnp.float32).astype(jnp.bfloat16)
    feature_block = lax.all_gather(hw_slice, "rep", axis=0, tiled=True)
    for level in range(digit_count):
        shifted = passed_along(feature_block, "blk", 1 << level)
        feature_block = jnp.where(rep_index // (1 << level) % 2 == 1, shifted, feature_block)
    tiles_per_part = feature_block.shape[0] // tile_size
    adjacency = [
        dense_adjacency(
            values_here[slot], rows_here[slot], cols_here[slot], counts_here[slot], tiles_per_part
        )
        for slot in range(pair_slots)
    ]
    aggregate = jnp.zeros(feature_block.shape, jnp.float32)
    for slot in range(pair_slots):
        aggregate = aggregate + jnp.dot(
            adjacency[slot], feature_block, preferred_element_type=jnp.float32
        )
        if slot + 1 < pair_slots:
            feature_block = passed_along(feature_block, "blk", replicas)
    aggregate_rows = lax.psum_scatter(
        aggregate.astype(jnp.bfloat16), "rep", scatter_dimension=0, tiled=True
    ).astype(jnp.float32)
    out, grad_rows = activation(aggregate_rows + bias, grad_out)
    grad_block = lax.all_gather(grad_rows, "rep", axis=0, tiled=True)
    partial_grad = jnp.zeros(grad_block.shape, jnp.float32)
    for slot in reversed(range(pair_slots)):
        partial_grad = partial_grad + lax.dot_general(
            adjacency[slot],
            grad_block,
            (((0,), (0,)), ((), ())),
            preferred_element_type=jnp.float32,
        )
        if slot > 0:
            partial_grad = passed_along(partial_grad.astype(jnp.bfloat16), "blk", -replicas).astype(
                partial_grad.dtype
            )
    for level in reversed(range(digit_count)):
        shifted = passed_along(partial_grad.astype(jnp.bfloat16), "blk", -(1 << level)).astype(
            partial_grad.dtype
        )
        partial_grad = jnp.where(rep_index // (1 << level) % 2 == 1, shifted, partial_grad)
    grad_hw = lax.psum_scatter(
        partial_grad.astype(jnp.bfloat16), "rep", scatter_dimension=0, tiled=True
    )
    grad_feats = lax.dot_general(
        grad_hw, weight, (((1,), (1,)), ((), ())), preferred_element_type=jnp.float32
    ).astype(jnp.bfloat16)
    weight_terms = lax.dot_general(
        feats, grad_hw, (((0,), (0,)), ((), ())), preferred_element_type=jnp.float32
    )
    weight_rows = weight.shape[0] // replicas
    bias_terms = jnp.sum(grad_rows.astype(jnp.float32), axis=0)
    weight_total, grad_bias = lax.psum((weight_terms, bias_terms), ("blk", "rep"))
    grad_weight = lax.dynamic_slice_in_dim(weight_total, rep_index * weight_rows, weight_rows, 0)
    return (out, grad_feats, grad_weight, grad_bias)


def solution(mesh):
    in_specs = (
        P(("blk", "rep"), None),
        P(),
        P(),
        P(("blk", "rep"), None),
        P("blk", "rep", None, None, None, None),
        P("blk", "rep", None, None),
        P("blk", "rep", None, None),
        P("blk", "rep", None),
    )
    out_specs = (P(("blk", "rep"), None), P(("blk", "rep"), None), P("rep", None), P())
    return jax.shard_map(body, mesh=mesh, in_specs=in_specs, out_specs=out_specs, check_vma=False)
```

profile of v0, /device:TPU:4, one launch (start us, length us, event | category | flops | bytes accessed | tf_op | source)
XLA Modules:
  0.0 1048.3 jit_solution(11181954026101608006)
XLA Ops:
  7.2 0.0 copy-start
  7.2 0.0 copy-start.6
  7.2 0.0 copy-start.7
  7.2 0.0 reduce-scatter.3.cloned.1.call-start
  7.2 0.8 copy-done
  8.1 0.9 convolution_convert_fusion.3
  9.0 22.4 %all_gather.6 = bf16[1024,256]{1,0:T(8,128)(2,1)S(1)} all-gather(bf16[64,256]{1,0:T(8,128)(2,1)S(1)} %convolution_convert_fusion.3), channel_id=1, replica_groups=mesh['blk'=32,'rep'=16] {'rep'}, dimensions={0}, use_global_device_ids=true | all-gather | bytes 557056 | tf_op jit(solution)/shard_map/all_gather | solution.py:48
  31.4 2.1 collective-permute-start
  33.5 0.0 copy-start.4
  33.5 21.3 %collective-permute-done = bf16[1024,256]{1,0:T(8,128)(2,1)S(1)} collective-permute-done((bf16[1024,256]{1,0:T(8,128)(2,1)S(1)}, bf16[1024,256]{1,0:T(8,128)(2,1)S(1)}, u32[]{:S(2)}, u32[]{:S(2)}) %collective-permute-start) | collective-permute-done | bytes 524320 | tf_op jit(solution)/shard_map/ppermute | solution.py:9
  54.8 0.1 broadcast_select_fusion
  54.9 1.9 collective-permute-start.1
  56.9 14.7 %collective-permute-done.1 = bf16[1024,256]{1,0:T(8,128)(2,1)S(1)} collective-permute-done((bf16[1024,256]{1,0:T(8,128)(2,1)S(1)}, bf16[1024,256]{1,0:T(8,128)(2,1)S(1)}, u32[]{:S(2)}, u32[]{:S(2)}) %collective-permute-start.1) | collective-permute-done | bytes 524320 | tf_op jit(solution)/shard_map/ppermute | solution.py:9
  71.6 0.1 broadcast_select_fusion.1
  71.7 1.9 collective-permute-start.2
  73.6 0.0 copy-done.6
  73.7 25.6 %collective-permute-done.2 = bf16[1024,256]{1,0:T(8,128)(2,1)S(1)} collective-permute-done((bf16[1024,256]{1,0:T(8,128)(2,1)S(1)}, bf16[1024,256]{1,0:T(8,128)(2,1)S(1)}, u32[]{:S(2)}, u32[]{:S(2)}) %collective-permute-start.2) | collective-permute-done | bytes 524320 | tf_op jit(solution)/shard_map/ppermute | solution.py:9
  99.3 0.1 broadcast_select_fusion.2
  99.4 2.4 collective-permute-start.3
  101.8 0.6 fusion.37
  102.4 0.6 iota_compare_fusion.3
  103.0 2.7 fusion.36
  105.7 41.7 %collective-permute-done.3 = bf16[1024,256]{1,0:T(8,128)(2,1)S(1)} collective-permute-done((bf16[1024,256]{1,0:T(8,128)(2,1)S(1)}, bf16[1024,256]{1,0:T(8,128)(2,1)S(1)}, u32[]{:S(2)}, u32[]{:S(2)}) %collective-permute-start.3) | collective-permute-done | bytes 524320 | tf_op jit(solution)/shard_map/ppermute | solution.py:9
  147.4 0.1 broadcast_select_fusion.3
  147.5 5.2 collective-permute-start.4
  152.7 1.7 convolution_convert_fusion.1
  154.4 0.7 iota_compare_fusion.2
  155.0 1.7 convolution_convert_fusion
  156.7 24.6 %collective-permute-done.4 = bf16[1024,256]{1,0:T(8,128)(2,1)S(1)} collective-permute-done((bf16[1024,256]{1,0:T(8,128)(2,1)S(1)}, bf16[1024,256]{1,0:T(8,128)(2,1)S(1)}, u32[]{:S(2)}, u32[]{:S(2)}) %collective-permute-start.4) | collective-permute-done | bytes 524320 | tf_op jit(solution)/shard_map/ppermute | solution.py:9
  181.4 0.7 fusion.2
  182.1 0.0 copy-start.3
  182.1 0.0 copy-start.5
  182.1 1.5 fusion.22
  183.6 0.0 reduce-scatter.3.cloned.1.call-update
  183.7 0.0 reduce-scatter.5.cloned.1.call-start
  183.7 109.7 %reduce-scatter.3.cloned.1.call-done = bf16[64,256]{1,0:T(8,128)(2,1)} async-done(((bf16[1024,256]{1,0:T(8,128)(2,1)}), bf16[64,256]{1,0:T(8,128)(2,1)}) %reduce-scatter.3.cloned.1.call-update) | async-done | bytes 32784 | tf_op jit(solution)/shard_map/reduce_scatter | solution.py:66
  293.4 1.4 convert_reduce_fusion
  294.9 21.4 %all_gather.7 = bf16[1024,256]{1,0:T(8,128)(2,1)S(1)} all-gather(bf16[64,256]{1,0:T(8,128)(2,1)S(1)} %get-tuple-element.9), channel_id=1, replica_groups=mesh['blk'=32,'rep'=16] {'rep'}, dimensions={0}, use_global_device_ids=true | all-gather | bytes 557056 | tf_op jit(solution)/shard_map/all_gather | solution.py:70
  316.3 2.4 fusion.19
  318.7 12.8 %collective-permute-start.5 = (bf16[1024,256]{1,0:T(8,128)(2,1)S(1)}, bf16[1024,256]{1,0:T(8,128)(2,1)S(1)}, u32[]{:S(2)}, u32[]{:S(2)}) collective-permute-start(bf16[1024,256]{1,0:T(8,128)(2,1)S(1)} %fusion.19), channel_id=1, source_target_pairs={{0,256},{16,272},{32,288},{48,304},{64,320},{80,336},{96,352},{112... | collective-permute-start | bytes 1572872 | tf_op jit(solution)/shard_map/ppermute | solution.py:9
  331.5 25.8 %collective-permute-done.5 = bf16[1024,256]{1,0:T(8,128)(2,1)S(1)} collective-permute-done((bf16[1024,256]{1,0:T(8,128)(2,1)S(1)}, bf16[1024,256]{1,0:T(8,128)(2,1)S(1)}, u32[]{:S(2)}, u32[]{:S(2)}) %collective-permute-start.5) | collective-permute-done | bytes 524320 | tf_op jit(solution)/shard_map/ppermute | solution.py:9
  357.3 0.8 fusion.25
  358.0 17.0 %collective-permute-start.6 = (bf16[1024,256]{1,0:T(8,128)(2,1)S(1)}, bf16[1024,256]{1,0:T(8,128)(2,1)S(1)}, u32[]{:S(2)}, u32[]{:S(2)}) collective-permute-start(bf16[1024,256]{1,0:T(8,128)(2,1)S(1)} %get-tuple-element.17), channel_id=1, source_target_pairs={{0,384},{16,400},{32,416},{48,432},{64,448},{80,464},{96,480},{112... | collective-permute-start | bytes 1572872 | tf_op jit(solution)/shard_map/ppermute | solution.py:9
  375.0 23.2 %collective-permute-done.6 = bf16[1024,256]{1,0:T(8,128)(2,1)S(1)} collective-permute-done((bf16[1024,256]{1,0:T(8,128)(2,1)S(1)}, bf16[1024,256]{1,0:T(8,128)(2,1)S(1)}, u32[]{:S(2)}, u32[]{:S(2)}) %collective-permute-start.6) | collective-permute-done | bytes 524320 | tf_op jit(solution)/shard_map/ppermute | solution.py:9
  398.2 0.2 convert_select_fusion.2
  398.4 25.2 %collective-permute-start.7 = (bf16[1024,256]{1,0:T(8,128)(2,1)S(1)}, bf16[1024,256]{1,0:T(8,128)(2,1)S(1)}, u32[]{:S(2)}, u32[]{:S(2)}) collective-permute-start(bf16[1024,256]{1,0:T(8,128)(2,1)S(1)} %convert_select_fusion.2), channel_id=1, source_target_pairs={{0,448},{16,464},{32,480},{48,496},{64,0},{80,16},{96,32},{112,48}... | collective-permute-start | bytes 1572872 | tf_op jit(solution)/shard_map/ppermute | solution.py:9
  423.7 26.4 %collective-permute-done.7 = bf16[1024,256]{1,0:T(8,128)(2,1)S(1)} collective-permute-done((bf16[1024,256]{1,0:T(8,128)(2,1)S(1)}, bf16[1024,256]{1,0:T(8,128)(2,1)S(1)}, u32[]{:S(2)}, u32[]{:S(2)}) %collective-permute-start.7) | collective-permute-done | bytes 524320 | tf_op jit(solution)/shard_map/ppermute | solution.py:9
  450.0 0.1 fusion.26
  450.2 1.9 collective-permute-start.8
  452.1 13.8 %collective-permute-done.8 = bf16[1024,256]{1,0:T(8,128)(2,1)S(1)} collective-permute-done((bf16[1024,256]{1,0:T(8,128)(2,1)S(1)}, bf16[1024,256]{1,0:T(8,128)(2,1)S(1)}, u32[]{:S(2)}, u32[]{:S(2)}) %collective-permute-start.8) | collective-permute-done | bytes 524320 | tf_op jit(solution)/shard_map/ppermute | solution.py:9
  465.9 0.2 fusion.27
  466.1 0.0 copy-start.2
  466.1 3.5 collective-permute-start.9
  469.6 11.4 %collective-permute-done.9 = bf16[1024,256]{1,0:T(8,128)(2,1)S(1)} collective-permute-done((bf16[1024,256]{1,0:T(8,128)(2,1)S(1)}, bf16[1024,256]{1,0:T(8,128)(2,1)S(1)}, u32[]{:S(2)}, u32[]{:S(2)}) %collective-permute-start.9) | collective-permute-done | bytes 524320 | tf_op jit(solution)/shard_map/ppermute | solution.py:9
  481.0 1.0 select_convert_fusion
  482.0 0.0 reduce-scatter.5.cloned.1.call-update
  482.1 0.0 all-reduce.2.cloned.1.call-start
  482.1 106.1 %psum.15 = f32[256]{0:T(256)} all-reduce(f32[256]{0:T(256)S(1)} %get-tuple-element.8), channel_id=1, replica_groups=mesh['blk'=32,'rep'=16] {'blk','rep'}, use_global_device_ids=true, to_apply=%region_4.5 | all-reduce | flops 256 | bytes 2048 | tf_op jit(solution)/shard_map/psum | solution.py:99
  588.2 1.7 convolution_bitcast_fusion
  589.9 0.0 all-reduce.2.cloned.1.call-update
  589.9 1.6 convolution_convert_fusion.2
  591.4 448.7 %all-reduce.2.cloned.1.call-done = f32[256,256]{0,1:T(8,128)} async-done(((f32[256,256]{0,1:T(8,128)}), f32[256,256]{0,1:T(8,128)}) %all-reduce.2.cloned.1.call-update) | async-done | bytes 262160 | tf_op jit(solution)/shard_map/psum | solution.py:99
  1040.1 1.0 constant_dynamic-slice_fusion
  1041.1 0.7 copy.12
  (9 shorter events, 0.0 us)
Async XLA Ops:
  7.2 0.9 copy-start
  7.2 66.4 %copy-start.6 = (s32[1,1,2,64]{3,2,1,0:T(2,128)S(1)}, s32[1,1,2,64]{3,2,1,0:T(2,128)}, u32[]{:S(2)}) copy-start(s32[1,1,2,64]{3,2,1,0:T(2,128)} %param.14) | copy-start | bytes 1540
  7.2 66.4 %copy-start.7 = (s32[1,1,2,64]{3,2,1,0:T(2,128)S(1)}, s32[1,1,2,64]{3,2,1,0:T(2,128)}, u32[]{:S(2)}) copy-start(s32[1,1,2,64]{3,2,1,0:T(2,128)} %param.13) | copy-start | bytes 1540
  7.2 286.2 %reduce-scatter.3.cloned.1.call-start = ((), (), s32[]{:S(2)}) async-start(), calls=%async_computation.2 | async-start | bytes 557056 | tf_op jit(solution)/shard_map/reduce_scatter | solution.py:66
  31.4 23.5 %collective-permute-start = (bf16[1024,256]{1,0:T(8,128)(2,1)S(1)}, bf16[1024,256]{1,0:T(8,128)(2,1)S(1)}, u32[]{:S(2)}, u32[]{:S(2)}) collective-permute-start(bf16[1024,256]{1,0:T(8,128)(2,1)S(1)} %all_gather.6), channel_id=1, source_target_pairs={{0,16},{16,32},{32,48},{48,64},{64,80},{80,96},{96,112},{112,128},... | collective-permute-start | bytes 1572872 | tf_op jit(solution)/shard_map/ppermute | solution.py:9
  33.5 68.3 %copy-start.4 = (s32[1,1,2]{2,1,0:T(1,128)S(1)}, s32[1,1,2]{2,1,0:T(1,128)}, u32[]{:S(2)}) copy-start(s32[1,1,2]{2,1,0:T(1,128)} %param.15) | copy-start | bytes 28
  54.9 16.7 %collective-permute-start.1 = (bf16[1024,256]{1,0:T(8,128)(2,1)S(1)}, bf16[1024,256]{1,0:T(8,128)(2,1)S(1)}, u32[]{:S(2)}, u32[]{:S(2)}) collective-permute-start(bf16[1024,256]{1,0:T(8,128)(2,1)S(1)} %broadcast_select_fusion), channel_id=1, source_target_pairs={{0,32},{16,48},{32,64},{48,80},{64,96},{80,112},{96,128},{112,144}... | collective-permute-start | bytes 1572872 | tf_op jit(solution)/shard_map/ppermute | solution.py:9
  71.7 27.6 %collective-permute-start.2 = (bf16[1024,256]{1,0:T(8,128)(2,1)S(1)}, bf16[1024,256]{1,0:T(8,128)(2,1)S(1)}, u32[]{:S(2)}, u32[]{:S(2)}) collective-permute-start(bf16[1024,256]{1,0:T(8,128)(2,1)S(1)} %broadcast_select_fusion.1), channel_id=1, source_target_pairs={{0,64},{16,80},{32,96},{48,112},{64,128},{80,144},{96,160},{112,17... | collective-permute-start | bytes 1572872 | tf_op jit(solution)/shard_map/ppermute | solution.py:9
  99.4 48.1 %collective-permute-start.3 = (bf16[1024,256]{1,0:T(8,128)(2,1)S(1)}, bf16[1024,256]{1,0:T(8,128)(2,1)S(1)}, u32[]{:S(2)}, u32[]{:S(2)}) collective-permute-start(bf16[1024,256]{1,0:T(8,128)(2,1)S(1)} %broadcast_select_fusion.2), channel_id=1, source_target_pairs={{0,128},{16,144},{32,160},{48,176},{64,192},{80,208},{96,224},{112... | collective-permute-start | bytes 1572872 | tf_op jit(solution)/shard_map/ppermute | solution.py:9
  147.5 33.9 %collective-permute-start.4 = (bf16[1024,256]{1,0:T(8,128)(2,1)S(1)}, bf16[1024,256]{1,0:T(8,128)(2,1)S(1)}, u32[]{:S(2)}, u32[]{:S(2)}) collective-permute-start(bf16[1024,256]{1,0:T(8,128)(2,1)S(1)} %broadcast_select_fusion.3), channel_id=1, source_target_pairs={{0,256},{16,272},{32,288},{48,304},{64,320},{80,336},{96,352},{112... | collective-permute-start | bytes 1572872 | tf_op jit(solution)/shard_map/ppermute | solution.py:9
  156.7 25.3 %copy-start.1 = (bf16[64,16384]{1,0:T(8,128)(2,1)}, bf16[64,16384]{1,0:T(8,128)(2,1)S(1)}, u32[]{:S(2)}) copy-start(bf16[64,16384]{1,0:T(8,128)(2,1)S(1)} %convolution_convert_fusion) | copy-start | bytes 6291460
  182.1 111.4 %copy-start.3 = (bf16[64,256]{1,0:T(8,128)(2,1)S(1)}, bf16[64,256]{1,0:T(8,128)(2,1)}, u32[]{:S(2)}) copy-start(bf16[64,256]{1,0:T(8,128)(2,1)} %param.11) | copy-start | bytes 98308
  182.1 111.3 %copy-start.5 = (f32[256]{0:T(256)S(1)}, f32[256]{0:T(256)}, u32[]{:S(2)}) copy-start(f32[256]{0:T(256)} %param.10) | copy-start | bytes 3076
  183.7 404.5 %reduce-scatter.5.cloned.1.call-start = ((), (), s32[]{:S(2)}) async-start(), calls=%async_computation.3 | async-start | bytes 557056 | tf_op jit(solution)/shard_map/reduce_scatter | solution.py:88
  318.7 38.6 %collective-permute-start.5 = (bf16[1024,256]{1,0:T(8,128)(2,1)S(1)}, bf16[1024,256]{1,0:T(8,128)(2,1)S(1)}, u32[]{:S(2)}, u32[]{:S(2)}) collective-permute-start(bf16[1024,256]{1,0:T(8,128)(2,1)S(1)} %fusion.19), channel_id=1, source_target_pairs={{0,256},{16,272},{32,288},{48,304},{64,320},{80,336},{96,352},{112... | collective-permute-start | bytes 1572872 | tf_op jit(solution)/shard_map/ppermute | solution.py:9
  358.0 40.2 %collective-permute-start.6 = (bf16[1024,256]{1,0:T(8,128)(2,1)S(1)}, bf16[1024,256]{1,0:T(8,128)(2,1)S(1)}, u32[]{:S(2)}, u32[]{:S(2)}) collective-permute-start(bf16[1024,256]{1,0:T(8,128)(2,1)S(1)} %get-tuple-element.17), channel_id=1, source_target_pairs={{0,384},{16,400},{32,416},{48,432},{64,448},{80,464},{96,480},{112... | collective-permute-start | bytes 1572872 | tf_op jit(solution)/shard_map/ppermute | solution.py:9
  398.4 51.6 %collective-permute-start.7 = (bf16[1024,256]{1,0:T(8,128)(2,1)S(1)}, bf16[1024,256]{1,0:T(8,128)(2,1)S(1)}, u32[]{:S(2)}, u32[]{:S(2)}) collective-permute-start(bf16[1024,256]{1,0:T(8,128)(2,1)S(1)} %convert_select_fusion.2), channel_id=1, source_target_pairs={{0,448},{16,464},{32,480},{48,496},{64,0},{80,16},{96,32},{112,48}... | collective-permute-start | bytes 1572872 | tf_op jit(solution)/shard_map/ppermute | solution.py:9
  450.2 15.7 %collective-permute-start.8 = (bf16[1024,256]{1,0:T(8,128)(2,1)S(1)}, bf16[1024,256]{1,0:T(8,128)(2,1)S(1)}, u32[]{:S(2)}, u32[]{:S(2)}) collective-permute-start(bf16[1024,256]{1,0:T(8,128)(2,1)S(1)} %fusion.26), channel_id=1, source_target_pairs={{0,480},{16,496},{32,0},{48,16},{64,32},{80,48},{96,64},{112,80},{... | collective-permute-start | bytes 1572872 | tf_op jit(solution)/shard_map/ppermute | solution.py:9
  466.1 122.1 %copy-start.2 = (bf16[64,256]{1,0:T(8,128)(2,1)S(1)}, bf16[64,256]{1,0:T(8,128)(2,1)}, u32[]{:S(2)}) copy-start(bf16[64,256]{1,0:T(8,128)(2,1)} %param.8) | copy-start | bytes 98308
  466.1 14.9 %collective-permute-start.9 = (bf16[1024,256]{1,0:T(8,128)(2,1)S(1)}, bf16[1024,256]{1,0:T(8,128)(2,1)S(1)}, u32[]{:S(2)}, u32[]{:S(2)}) collective-permute-start(bf16[1024,256]{1,0:T(8,128)(2,1)S(1)} %fusion.27), channel_id=1, source_target_pairs={{0,496},{16,0},{32,16},{48,32},{64,48},{80,64},{96,80},{112,96},{1... | collective-permute-start | bytes 1572872 | tf_op jit(solution)/shard_map/ppermute | solution.py:9
  482.1 558.0 %all-reduce.2.cloned.1.call-start = ((), (), s32[]{:S(2)}) async-start(), calls=%async_computation.4 | async-start | bytes 524288 | tf_op jit(solution)/shard_map/psum | solution.py:99
Sparse Core Ops, SparseCore 0:
  183.8 109.6 reduce-scatter.2
  482.2 85.5 reduce-scatter.4
  590.0 450.0 all-reduce.1
where the time goes:
time: 1050 us
  waiting for transfers between devices  787 us (75%)
  blocking collectives  150 us (14%)
  starting transfers between devices  74 us (7%)
  between operations  14.1 us (1%)
  matrix products  12.9 us (1%)
    psum x1, waiting for transfers between devices, body(): lax.psum((weight_terms, bias_terms), ('blk', 'rep'))  449 us
    ppermute x10, waiting for transfers between devices, passed_along(): lax.ppermute(x, axis, [(i, (i + by) % devices) for i in range(devices)])  229 us
    reduce_scatter x1, waiting for transfers between devices, body(): lax.psum_scatter(aggregate.astype(jnp.bfloat16), 'rep', scatter_dimension...  110 us
    psum x1, blocking collectives, body(): lax.psum((weight_terms, bias_terms), ('blk', 'rep'))  106 us
    ppermute x10, starting transfers between devices, passed_along(): lax.ppermute(x, axis, [(i, (i + by) % devices) for i in range(devices)])  73.9 us
    all_gather x1, blocking collectives, body(): feature_block = lax.all_gather(hw_slice, 'rep', axis=0, tiled=True)  22.4 us
    all_gather x1, blocking collectives, body(): grad_block = lax.all_gather(grad_rows, 'rep', axis=0, tiled=True)  21.4 us
  transfers between devices with their start and end apart: 13, of which 12 were waited for; matrix products, arithmetic and copies ran while one was open for 1% of the time, Pallas kernels for 0%

commit v1 on v0

--- a/solution.py
+++ b/solution.py
@@ -96,7 +96,7 @@
     )
     weight_rows = weight.shape[0] // replicas
     bias_terms = jnp.sum(grad_rows.astype(jnp.float32), axis=0)
-    weight_total, grad_bias = lax.psum((weight_terms, bias_terms), ("blk", "rep"))
+    weight_total, grad_bias = lax.psum(lax.psum((weight_terms, bias_terms), "blk"), "rep")
     grad_weight = lax.dynamic_slice_in_dim(weight_total, rep_index * weight_rows, weight_rows, 0)
     return (out, grad_feats, grad_weight, grad_bias)
 

time: 1050 us -> 997 us (0.950)
  the two profiles are of different devices: /device:TPU:4 before, /device:TPU:1 now
where the time goes in v1:
time: 997 us; the launch traced here: 996 us
  waiting for transfers between devices  710 us (71%)
  blocking collectives  170 us (17%)
  starting transfers between devices  78.7 us (8%)
  between operations  14.1 us (1%)
  matrix products  12.9 us (1%)
    psum x1, waiting for transfers between devices, body(): lax.psum((weight_terms, bias_terms), 'blk')  243 us
    ppermute x10, waiting for transfers between devices, passed_along(): lax.ppermute(x, axis, [(i, (i + by) % devices) for i in range(devices)])  226 us
    reduce_scatter x1, waiting for transfers between devices, body(): lax.psum_scatter(aggregate.astype(jnp.bfloat16), 'rep', scatter_dimension...  101 us
    reduce_scatter x1, waiting for transfers between devices, body(): lax.psum_scatter(partial_grad.astype(jnp.bfloat16), 'rep', scatter_dimens...  83.2 us
    ppermute x10, starting transfers between devices, passed_along(): lax.ppermute(x, axis, [(i, (i + by) % devices) for i in range(devices)])  78.6 us
    psum x1, blocking collectives, body(): lax.psum(lax.psum((weight_terms, bias_terms), 'blk'), 'rep')  67.6 us
    psum x1, waiting for transfers between devices, body(): lax.psum(lax.psum((weight_terms, bias_terms), 'blk'), 'rep')  56.2 us
    psum x1, blocking collectives, body(): lax.psum((weight_terms, bias_terms), 'blk')  49.3 us
  transfers between devices with their start and end apart: 14, of which 14 were waited for; matrix products, arithmetic and copies ran while one was open for 1% of the time, Pallas kernels for 0%

profile of v1, /device:TPU:1, one launch (start us, length us, event | category | flops | bytes accessed | tf_op | source)
XLA Modules:
  0.0 995.7 jit_solution(13684550589999004910)
XLA Ops:
  7.2 0.0 copy-start
  7.2 0.0 reduce-scatter.3.cloned.1.call-start
  7.2 0.8 copy-done
  8.1 0.9 convolution_convert_fusion.3
  9.0 27.2 %all_gather.6 = bf16[1024,256]{1,0:T(8,128)(2,1)S(1)} all-gather(bf16[64,256]{1,0:T(8,128)(2,1)S(1)} %convolution_convert_fusion.3), channel_id=1, replica_groups=mesh['blk'=32,'rep'=16] {'rep'}, dimensions={0}, use_global_device_ids=true | all-gather | bytes 557056 | tf_op jit(solution)/shard_map/all_gather | solution.py:48
  36.2 2.2 collective-permute-start
  38.5 0.0 copy-start.4
  38.5 21.0 %collective-permute-done = bf16[1024,256]{1,0:T(8,128)(2,1)S(1)} collective-permute-done((bf16[1024,256]{1,0:T(8,128)(2,1)S(1)}, bf16[1024,256]{1,0:T(8,128)(2,1)S(1)}, u32[]{:S(2)}, u32[]{:S(2)}) %collective-permute-start) | collective-permute-done | bytes 524320 | tf_op jit(solution)/shard_map/ppermute | solution.py:9
  59.5 0.1 broadcast_select_fusion
  59.6 1.9 collective-permute-start.1
  61.5 13.9 %collective-permute-done.1 = bf16[1024,256]{1,0:T(8,128)(2,1)S(1)} collective-permute-done((bf16[1024,256]{1,0:T(8,128)(2,1)S(1)}, bf16[1024,256]{1,0:T(8,128)(2,1)S(1)}, u32[]{:S(2)}, u32[]{:S(2)}) %collective-permute-start.1) | collective-permute-done | bytes 524320 | tf_op jit(solution)/shard_map/ppermute | solution.py:9
  75.4 0.1 broadcast_select_fusion.1
  75.5 1.9 collective-permute-start.2
  77.4 25.0 %collective-permute-done.2 = bf16[1024,256]{1,0:T(8,128)(2,1)S(1)} collective-permute-done((bf16[1024,256]{1,0:T(8,128)(2,1)S(1)}, bf16[1024,256]{1,0:T(8,128)(2,1)S(1)}, u32[]{:S(2)}, u32[]{:S(2)}) %collective-permute-start.2) | collective-permute-done | bytes 524320 | tf_op jit(solution)/shard_map/ppermute | solution.py:9
  102.4 0.1 broadcast_select_fusion.2
  102.5 2.9 collective-permute-start.3
  105.4 0.6 fusion.37
  106.0 0.6 iota_compare_fusion.3
  106.7 2.7 fusion.36
  109.4 40.6 %collective-permute-done.3 = bf16[1024,256]{1,0:T(8,128)(2,1)S(1)} collective-permute-done((bf16[1024,256]{1,0:T(8,128)(2,1)S(1)}, bf16[1024,256]{1,0:T(8,128)(2,1)S(1)}, u32[]{:S(2)}, u32[]{:S(2)}) %collective-permute-start.3) | collective-permute-done | bytes 524320 | tf_op jit(solution)/shard_map/ppermute | solution.py:9
  150.0 0.1 broadcast_select_fusion.3
  150.1 1.9 collective-permute-start.4
  152.0 1.7 convolution_convert_fusion.1
  153.7 0.7 iota_compare_fusion.2
  154.4 1.7 convolution_convert_fusion
  156.1 34.6 %collective-permute-done.4 = bf16[1024,256]{1,0:T(8,128)(2,1)S(1)} collective-permute-done((bf16[1024,256]{1,0:T(8,128)(2,1)S(1)}, bf16[1024,256]{1,0:T(8,128)(2,1)S(1)}, u32[]{:S(2)}, u32[]{:S(2)}) %collective-permute-start.4) | collective-permute-done | bytes 524320 | tf_op jit(solution)/shard_map/ppermute | solution.py:9
  190.7 0.7 fusion.2
  191.5 0.0 copy-start.5
  191.5 1.5 fusion.22
  193.0 0.0 reduce-scatter.3.cloned.1.call-update
  193.0 0.0 reduce-scatter.5.cloned.1.call-start
  193.1 100.8 %reduce-scatter.3.cloned.1.call-done = bf16[64,256]{1,0:T(8,128)(2,1)} async-done(((bf16[1024,256]{1,0:T(8,128)(2,1)}), bf16[64,256]{1,0:T(8,128)(2,1)}) %reduce-scatter.3.cloned.1.call-update) | async-done | bytes 32784 | tf_op jit(solution)/shard_map/reduce_scatter | solution.py:66
  293.9 1.4 convert_reduce_fusion
  295.3 25.5 %all_gather.7 = bf16[1024,256]{1,0:T(8,128)(2,1)S(1)} all-gather(bf16[64,256]{1,0:T(8,128)(2,1)S(1)} %get-tuple-element.9), channel_id=1, replica_groups=mesh['blk'=32,'rep'=16] {'rep'}, dimensions={0}, use_global_device_ids=true | all-gather | bytes 557056 | tf_op jit(solution)/shard_map/all_gather | solution.py:70
  320.8 2.4 fusion.19
  323.1 12.5 %collective-permute-start.5 = (bf16[1024,256]{1,0:T(8,128)(2,1)S(1)}, bf16[1024,256]{1,0:T(8,128)(2,1)S(1)}, u32[]{:S(2)}, u32[]{:S(2)}) collective-permute-start(bf16[1024,256]{1,0:T(8,128)(2,1)S(1)} %fusion.19), channel_id=1, source_target_pairs={{0,256},{16,272},{32,288},{48,304},{64,320},{80,336},{96,352},{112... | collective-permute-start | bytes 1572872 | tf_op jit(solution)/shard_map/ppermute | solution.py:9
  335.6 25.3 %collective-permute-done.5 = bf16[1024,256]{1,0:T(8,128)(2,1)S(1)} collective-permute-done((bf16[1024,256]{1,0:T(8,128)(2,1)S(1)}, bf16[1024,256]{1,0:T(8,128)(2,1)S(1)}, u32[]{:S(2)}, u32[]{:S(2)}) %collective-permute-start.5) | collective-permute-done | bytes 524320 | tf_op jit(solution)/shard_map/ppermute | solution.py:9
  360.9 0.8 fusion.25
  361.7 16.5 %collective-permute-start.6 = (bf16[1024,256]{1,0:T(8,128)(2,1)S(1)}, bf16[1024,256]{1,0:T(8,128)(2,1)S(1)}, u32[]{:S(2)}, u32[]{:S(2)}) collective-permute-start(bf16[1024,256]{1,0:T(8,128)(2,1)S(1)} %get-tuple-element.17), channel_id=1, source_target_pairs={{0,384},{16,400},{32,416},{48,432},{64,448},{80,464},{96,480},{112... | collective-permute-start | bytes 1572872 | tf_op jit(solution)/shard_map/ppermute | solution.py:9
  378.2 17.5 %collective-permute-done.6 = bf16[1024,256]{1,0:T(8,128)(2,1)S(1)} collective-permute-done((bf16[1024,256]{1,0:T(8,128)(2,1)S(1)}, bf16[1024,256]{1,0:T(8,128)(2,1)S(1)}, u32[]{:S(2)}, u32[]{:S(2)}) %collective-permute-start.6) | collective-permute-done | bytes 524320 | tf_op jit(solution)/shard_map/ppermute | solution.py:9
  395.7 0.2 convert_select_fusion.2
  395.9 32.9 %collective-permute-start.7 = (bf16[1024,256]{1,0:T(8,128)(2,1)S(1)}, bf16[1024,256]{1,0:T(8,128)(2,1)S(1)}, u32[]{:S(2)}, u32[]{:S(2)}) collective-permute-start(bf16[1024,256]{1,0:T(8,128)(2,1)S(1)} %convert_select_fusion.2), channel_id=1, source_target_pairs={{0,448},{16,464},{32,480},{48,496},{64,0},{80,16},{96,32},{112,48}... | collective-permute-start | bytes 1572872 | tf_op jit(solution)/shard_map/ppermute | solution.py:9
  428.7 25.4 %collective-permute-done.7 = bf16[1024,256]{1,0:T(8,128)(2,1)S(1)} collective-permute-done((bf16[1024,256]{1,0:T(8,128)(2,1)S(1)}, bf16[1024,256]{1,0:T(8,128)(2,1)S(1)}, u32[]{:S(2)}, u32[]{:S(2)}) %collective-permute-start.7) | collective-permute-done | bytes 524320 | tf_op jit(solution)/shard_map/ppermute | solution.py:9
  454.2 0.1 fusion.26
  454.3 1.9 collective-permute-start.8
  456.2 13.0 %collective-permute-done.8 = bf16[1024,256]{1,0:T(8,128)(2,1)S(1)} collective-permute-done((bf16[1024,256]{1,0:T(8,128)(2,1)S(1)}, bf16[1024,256]{1,0:T(8,128)(2,1)S(1)}, u32[]{:S(2)}, u32[]{:S(2)}) %collective-permute-start.8) | collective-permute-done | bytes 524320 | tf_op jit(solution)/shard_map/ppermute | solution.py:9
  469.2 0.2 fusion.27
  469.4 3.9 collective-permute-start.9
  473.3 10.2 %collective-permute-done.9 = bf16[1024,256]{1,0:T(8,128)(2,1)S(1)} collective-permute-done((bf16[1024,256]{1,0:T(8,128)(2,1)S(1)}, bf16[1024,256]{1,0:T(8,128)(2,1)S(1)}, u32[]{:S(2)}, u32[]{:S(2)}) %collective-permute-start.9) | collective-permute-done | bytes 524320 | tf_op jit(solution)/shard_map/ppermute | solution.py:9
  483.5 1.0 select_convert_fusion
  484.5 0.0 reduce-scatter.5.cloned.1.call-update
  484.6 0.0 all-reduce.3.cloned.1.call-start
  484.6 83.2 %reduce-scatter.5.cloned.1.call-done = bf16[64,256]{1,0:T(8,128)(2,1)} async-done(((bf16[1024,256]{1,0:T(8,128)(2,1)}), bf16[64,256]{1,0:T(8,128)(2,1)}) %reduce-scatter.5.cloned.1.call-update) | async-done | bytes 32784 | tf_op jit(solution)/shard_map/reduce_scatter | solution.py:88
  567.9 1.7 convolution_bitcast_fusion
  569.5 0.0 all-reduce.3.cloned.1.call-update
  569.6 0.0 all-reduce.5.cloned.1.call-start
  569.6 243.1 %all-reduce.3.cloned.1.call-done = f32[256,256]{0,1:T(8,128)} async-done(((f32[256,256]{0,1:T(8,128)}), f32[256,256]{0,1:T(8,128)}) %all-reduce.3.cloned.1.call-update) | async-done | bytes 262160 | tf_op jit(solution)/shard_map/psum | solution.py:99
  812.7 0.0 all-reduce.5.cloned.1.call-update
  812.7 49.3 %psum.30 = f32[256]{0:T(256)S(1)} all-reduce(f32[256]{0:T(256)S(1)} %get-tuple-element.8), channel_id=1, replica_groups=mesh['blk'=32,'rep'=16] {'blk'}, use_global_device_ids=true, to_apply=%region_5.6 | all-reduce | flops 256 | bytes 2048 | tf_op jit(solution)/shard_map/psum | solution.py:99
  862.1 67.6 %psum.31 = f32[256]{0:T(256)} all-reduce(f32[256]{0:T(256)S(1)} %psum.30), channel_id=1, replica_groups=mesh['blk'=32,'rep'=16] {'rep'}, use_global_device_ids=true, to_apply=%region_6.7 | all-reduce | flops 256 | bytes 2048 | tf_op jit(solution)/shard_map/psum | solution.py:99
  929.7 1.6 convolution_convert_fusion.2
  931.3 56.2 %all-reduce.5.cloned.1.call-done = f32[256,256]{0,1:T(8,128)} async-done(((f32[256,256]{0,1:T(8,128)}), f32[256,256]{0,1:T(8,128)}) %all-reduce.5.cloned.1.call-update) | async-done | bytes 262160 | tf_op jit(solution)/shard_map/psum | solution.py:99
  987.5 1.0 constant_dynamic-slice_fusion
  988.5 0.7 copy.12
  (13 shorter events, 0.0 us)
Async XLA Ops:
  7.2 0.9 copy-start
  7.2 70.2 %copy-start.6 = (s32[1,1,2,64]{3,2,1,0:T(2,128)S(1)}, s32[1,1,2,64]{3,2,1,0:T(2,128)}, u32[]{:S(2)}) copy-start(s32[1,1,2,64]{3,2,1,0:T(2,128)} %param.14) | copy-start | bytes 1540
  7.2 70.2 %copy-start.7 = (s32[1,1,2,64]{3,2,1,0:T(2,128)S(1)}, s32[1,1,2,64]{3,2,1,0:T(2,128)}, u32[]{:S(2)}) copy-start(s32[1,1,2,64]{3,2,1,0:T(2,128)} %param.13) | copy-start | bytes 1540
  7.2 286.7 %reduce-scatter.3.cloned.1.call-start = ((), (), s32[]{:S(2)}) async-start(), calls=%async_computation.2 | async-start | bytes 557056 | tf_op jit(solution)/shard_map/reduce_scatter | solution.py:66
  36.2 23.3 %collective-permute-start = (bf16[1024,256]{1,0:T(8,128)(2,1)S(1)}, bf16[1024,256]{1,0:T(8,128)(2,1)S(1)}, u32[]{:S(2)}, u32[]{:S(2)}) collective-permute-start(bf16[1024,256]{1,0:T(8,128)(2,1)S(1)} %all_gather.6), channel_id=1, source_target_pairs={{0,16},{16,32},{32,48},{48,64},{64,80},{80,96},{96,112},{112,128},... | collective-permute-start | bytes 1572872 | tf_op jit(solution)/shard_map/ppermute | solution.py:9
  38.5 66.9 %copy-start.4 = (s32[1,1,2]{2,1,0:T(1,128)S(1)}, s32[1,1,2]{2,1,0:T(1,128)}, u32[]{:S(2)}) copy-start(s32[1,1,2]{2,1,0:T(1,128)} %param.15) | copy-start | bytes 28
  59.6 15.8 %collective-permute-start.1 = (bf16[1024,256]{1,0:T(8,128)(2,1)S(1)}, bf16[1024,256]{1,0:T(8,128)(2,1)S(1)}, u32[]{:S(2)}, u32[]{:S(2)}) collective-permute-start(bf16[1024,256]{1,0:T(8,128)(2,1)S(1)} %broadcast_select_fusion), channel_id=1, source_target_pairs={{0,32},{16,48},{32,64},{48,80},{64,96},{80,112},{96,128},{112,144}... | collective-permute-start | bytes 1572872 | tf_op jit(solution)/shard_map/ppermute | solution.py:9
  75.5 27.0 %collective-permute-start.2 = (bf16[1024,256]{1,0:T(8,128)(2,1)S(1)}, bf16[1024,256]{1,0:T(8,128)(2,1)S(1)}, u32[]{:S(2)}, u32[]{:S(2)}) collective-permute-start(bf16[1024,256]{1,0:T(8,128)(2,1)S(1)} %broadcast_select_fusion.1), channel_id=1, source_target_pairs={{0,64},{16,80},{32,96},{48,112},{64,128},{80,144},{96,160},{112,17... | collective-permute-start | bytes 1572872 | tf_op jit(solution)/shard_map/ppermute | solution.py:9
  102.5 47.5 %collective-permute-start.3 = (bf16[1024,256]{1,0:T(8,128)(2,1)S(1)}, bf16[1024,256]{1,0:T(8,128)(2,1)S(1)}, u32[]{:S(2)}, u32[]{:S(2)}) collective-permute-start(bf16[1024,256]{1,0:T(8,128)(2,1)S(1)} %broadcast_select_fusion.2), channel_id=1, source_target_pairs={{0,128},{16,144},{32,160},{48,176},{64,192},{80,208},{96,224},{112... | collective-permute-start | bytes 1572872 | tf_op jit(solution)/shard_map/ppermute | solution.py:9
  150.1 40.6 %collective-permute-start.4 = (bf16[1024,256]{1,0:T(8,128)(2,1)S(1)}, bf16[1024,256]{1,0:T(8,128)(2,1)S(1)}, u32[]{:S(2)}, u32[]{:S(2)}) collective-permute-start(bf16[1024,256]{1,0:T(8,128)(2,1)S(1)} %broadcast_select_fusion.3), channel_id=1, source_target_pairs={{0,256},{16,272},{32,288},{48,304},{64,320},{80,336},{96,352},{112... | collective-permute-start | bytes 1572872 | tf_op jit(solution)/shard_map/ppermute | solution.py:9
  156.1 35.4 %copy-start.1 = (bf16[64,16384]{1,0:T(8,128)(2,1)}, bf16[64,16384]{1,0:T(8,128)(2,1)S(1)}, u32[]{:S(2)}) copy-start(bf16[64,16384]{1,0:T(8,128)(2,1)S(1)} %convolution_convert_fusion) | copy-start | bytes 6291460
  191.5 102.4 %copy-start.3 = (bf16[64,256]{1,0:T(8,128)(2,1)S(1)}, bf16[64,256]{1,0:T(8,128)(2,1)}, u32[]{:S(2)}) copy-start(bf16[64,256]{1,0:T(8,128)(2,1)} %param.11) | copy-start | bytes 98308
  191.5 102.4 %copy-start.5 = (f32[256]{0:T(256)S(1)}, f32[256]{0:T(256)}, u32[]{:S(2)}) copy-start(f32[256]{0:T(256)} %param.10) | copy-start | bytes 3076
  193.0 374.8 %reduce-scatter.5.cloned.1.call-start = ((), (), s32[]{:S(2)}) async-start(), calls=%async_computation.3 | async-start | bytes 557056 | tf_op jit(solution)/shard_map/reduce_scatter | solution.py:88
  323.1 37.8 %collective-permute-start.5 = (bf16[1024,256]{1,0:T(8,128)(2,1)S(1)}, bf16[1024,256]{1,0:T(8,128)(2,1)S(1)}, u32[]{:S(2)}, u32[]{:S(2)}) collective-permute-start(bf16[1024,256]{1,0:T(8,128)(2,1)S(1)} %fusion.19), channel_id=1, source_target_pairs={{0,256},{16,272},{32,288},{48,304},{64,320},{80,336},{96,352},{112... | collective-permute-start | bytes 1572872 | tf_op jit(solution)/shard_map/ppermute | solution.py:9
  361.7 34.0 %collective-permute-start.6 = (bf16[1024,256]{1,0:T(8,128)(2,1)S(1)}, bf16[1024,256]{1,0:T(8,128)(2,1)S(1)}, u32[]{:S(2)}, u32[]{:S(2)}) collective-permute-start(bf16[1024,256]{1,0:T(8,128)(2,1)S(1)} %get-tuple-element.17), channel_id=1, source_target_pairs={{0,384},{16,400},{32,416},{48,432},{64,448},{80,464},{96,480},{112... | collective-permute-start | bytes 1572872 | tf_op jit(solution)/shard_map/ppermute | solution.py:9
  395.9 58.3 %collective-permute-start.7 = (bf16[1024,256]{1,0:T(8,128)(2,1)S(1)}, bf16[1024,256]{1,0:T(8,128)(2,1)S(1)}, u32[]{:S(2)}, u32[]{:S(2)}) collective-permute-start(bf16[1024,256]{1,0:T(8,128)(2,1)S(1)} %convert_select_fusion.2), channel_id=1, source_target_pairs={{0,448},{16,464},{32,480},{48,496},{64,0},{80,16},{96,32},{112,48}... | collective-permute-start | bytes 1572872 | tf_op jit(solution)/shard_map/ppermute | solution.py:9
  454.3 14.9 %collective-permute-start.8 = (bf16[1024,256]{1,0:T(8,128)(2,1)S(1)}, bf16[1024,256]{1,0:T(8,128)(2,1)S(1)}, u32[]{:S(2)}, u32[]{:S(2)}) collective-permute-start(bf16[1024,256]{1,0:T(8,128)(2,1)S(1)} %fusion.26), channel_id=1, source_target_pairs={{0,480},{16,496},{32,0},{48,16},{64,32},{80,48},{96,64},{112,80},{... | collective-permute-start | bytes 1572872 | tf_op jit(solution)/shard_map/ppermute | solution.py:9
  469.4 98.5 %copy-start.2 = (bf16[64,256]{1,0:T(8,128)(2,1)S(1)}, bf16[64,256]{1,0:T(8,128)(2,1)}, u32[]{:S(2)}) copy-start(bf16[64,256]{1,0:T(8,128)(2,1)} %param.8) | copy-start | bytes 98308
  469.4 14.1 %collective-permute-start.9 = (bf16[1024,256]{1,0:T(8,128)(2,1)S(1)}, bf16[1024,256]{1,0:T(8,128)(2,1)S(1)}, u32[]{:S(2)}, u32[]{:S(2)}) collective-permute-start(bf16[1024,256]{1,0:T(8,128)(2,1)S(1)} %fusion.27), channel_id=1, source_target_pairs={{0,496},{16,0},{32,16},{48,32},{64,48},{80,64},{96,80},{112,96},{1... | collective-permute-start | bytes 1572872 | tf_op jit(solution)/shard_map/ppermute | solution.py:9
  484.6 328.1 %all-reduce.3.cloned.1.call-start = ((), (), s32[]{:S(2)}) async-start(), calls=%async_computation.4 | async-start | bytes 524288 | tf_op jit(solution)/shard_map/psum | solution.py:99
  569.6 417.9 %all-reduce.5.cloned.1.call-start = ((), (), s32[]{:S(2)}) async-start(), calls=%async_computation.5 | async-start | bytes 524288 | tf_op jit(solution)/shard_map/psum | solution.py:99
Sparse Core Ops, SparseCore 0:
  193.1 100.7 reduce-scatter.2
  484.7 83.1 reduce-scatter.4
  570.8 241.8 all-reduce.2
  815.7 171.7 all-reduce.4
